TPU v7x, 32 devices: a whole 2x2x4 slice. The times are simulated.
32 devices in a mesh: group: 2 (over x), node: 16 (over z, y, core).
Axes of the slice: x: 2, y: 2, z: 4, core: 2. Of those that a mesh axis runs over, the one named last changes fastest.
Arguments:
- states: bfloat16 [512, 2048], P(('group', 'node')), parts along dimension 0, may hold values from -400 to 400
- norm_gain: float32 [2048], replicated, may hold values from 0.5 to 1.5
- picks: int32 [512, 8], P(('group', 'node')), parts along dimension 0, may hold values from 0 to 15, all different within a row; in each aligned block of 16 rows (0 to 15, 16 to 31, ...) at most 16 rows name the same one
- gate_weights: float32 [512, 8], P(('group', 'node')), parts along dimension 0, may hold values from 0.05 to 1
- w_gate: bfloat16 [16, 2048, 768], P('node'), may hold values from -0.125 to 0.125
- w_up: bfloat16 [16, 2048, 768], P('node'), may hold values from -0.125 to 0.125
- w_down: bfloat16 [16, 768, 2048], P('node'), may hold values from -0.21875 to 0.21875
- queries: bfloat16 [128, 4096], P(('group', 'node')), parts along dimension 0, may hold values from -88 to 88
- keys: bfloat16 [128, 256, 512], P(('group', 'node')), parts along dimension 0, may hold values from -4 to 4
- values: bfloat16 [128, 256, 512], P(('group', 'node')), parts along dimension 0, may hold values from -4 to 4
- incoming_keys: bfloat16 [128, 512], P(('group', 'node')), parts along dimension 0, may hold values from -4 to 4
- incoming_values: bfloat16 [128, 512], P(('group', 'node')), parts along dimension 0, may hold values from -4 to 4
- lengths: int32 [128], P(('group', 'node')), parts along dimension 0, may hold values from 32 to 256, as said below
Outputs:
- moe_output: bfloat16 [512, 2048], P(('group', 'node')), parts along dimension 0
- attention_output: bfloat16 [128, 4096], P(('group', 'node')), parts along dimension 0
There are 2 independent parts, one for each index of `group`. A program takes and returns all parts, laid end to end along the dimension named above; an argument that names none is the same for every part. Nothing has to cross between parts.
Inputs may be any that keep to these rules, and one draw needn't show every extreme that they name: Each token picks 8 different experts; among the 16 tokens of one device no expert is picked by more than 16 tokens, a bound that some block reaches. `lengths`: the first request of each device holds 256 cached tokens.
All inputs are finite; a program needn't handle non-finite values.
Results may differ from a plain program's by a relative error of at most 0.0085.
Values may be sent and summed in bfloat16 or wider, within the bound.
No kernel may reach another device: no remote copies, remote signals or barrier semaphores. Data moves between devices by JAX's collectives and lax.ppermute only.
A program may use at most 64 MiB of HBM per device.

v0:
```python
import math
import jax
import jax.numpy as jnp
from jax import lax
from jax.sharding import PartitionSpec as P

QUERY_HEADS = 32
KEY_VALUE_HEADS = 4
HEAD_WIDTH = 128
TOPK = 8
TOK_DEV = 16


def expert_block(received, w_gate, w_up, w_down):
    peers = lax.axis_size("node")
    local_experts = w_gate.shape[0]
    slot_count = received.shape[1]
    features = received.shape[2]
    grouped = received.reshape(peers, local_experts, slot_count, features)
    gate_part = jnp.einsum("nesd,edf->nesf", grouped, w_gate, preferred_element_type=jnp.float32)
    up_part = jnp.einsum("nesd,edf->nesf", grouped, w_up, preferred_element_type=jnp.float32)
    inner = (jax.nn.silu(gate_part) * up_part).astype(jnp.bfloat16)
    produced = jnp.einsum(
        "nesf,efd->nesd", inner, w_down, preferred_element_type=jnp.float32
    ).astype(jnp.bfloat16)
    return produced.reshape(peers * local_experts, slot_count, features)


def route_block(normed, picks, gate_weights, w_gate, w_up, w_down, capacity):
    rows_here = picks.shape[0]
    picks_here = picks.shape[1]
    experts_all = w_gate.shape[0] * lax.axis_size("node")
    features = normed.shape[1]
    flattened = picks.reshape(-1)
    expert_ids = jnp.arange(experts_all, dtype=jnp.int32)
    onehot = (flattened[:, None] == expert_ids[None, :]).astype(jnp.int32)
    earlier = jnp.cumsum(onehot, axis=0) - onehot
    slot_of = jnp.sum(earlier * onehot, axis=1)
    target = flattened * capacity + slot_of
    layout = jnp.arange(experts_all * capacity, dtype=jnp.int32)
    placed = jnp.sum(
        (layout[:, None, None] == target.reshape(rows_here, picks_here)[None, :, :]).astype(
            jnp.int32
        ),
        axis=2,
    )
    outgoing = jnp.dot(placed.astype(jnp.bfloat16), normed, preferred_element_type=jnp.float32)
    outgoing = outgoing.astype(jnp.bfloat16).reshape(experts_all, capacity, features)
    produced = expert_block(
        lax.all_to_all(outgoing, "node", split_axis=0, concat_axis=0, tiled=True),
        w_gate,
        w_up,
        w_down,
    )
    returned = lax.all_to_all(produced, "node", split_axis=0, concat_axis=0, tiled=True)
    gathered = jnp.take(returned.reshape(experts_all * capacity, features), target, axis=0)
    gathered = gathered.reshape(rows_here, picks_here, features)
    shares = gate_weights / jnp.sum(gate_weights, axis=1, keepdims=True)
    return jnp.einsum("tk,tkd->td", shares, gathered.astype(jnp.float32)).astype(jnp.bfloat16)


def dense_block(normed, picks, gate_weights, w_gate, w_up, w_down):
    local_experts = w_gate.shape[0]
    node_index = lax.axis_index("node")
    experts_all = local_experts * lax.axis_size("node")
    shares = gate_weights / jnp.sum(gate_weights, axis=1, keepdims=True)
    expert_ids = jnp.arange(experts_all, dtype=jnp.int32)
    chosen = picks[:, :, None] == expert_ids[None, None, :]
    dense_shares = jnp.sum(jnp.where(chosen, shares[:, :, None], 0.0), axis=1)
    every_row = lax.all_gather(normed, "node", axis=0, tiled=True)
    every_share = lax.all_gather(dense_shares, "node", axis=0, tiled=True)
    own_shares = lax.dynamic_slice_in_dim(
        every_share, node_index * local_experts, local_experts, axis=1
    )
    summed = None
    for expert in range(local_experts):
        gate_part = jnp.dot(every_row, w_gate[expert], preferred_element_type=jnp.float32)
        up_part = jnp.dot(every_row, w_up[expert], preferred_element_type=jnp.float32)
        inner = (jax.nn.silu(gate_part) * up_part).astype(jnp.bfloat16)
        produced = jnp.dot(inner, w_down[expert], preferred_element_type=jnp.float32).astype(
            jnp.bfloat16
        )
        column = own_shares[:, expert : expert + 1]
        weighted = jnp.where(column != 0.0, column * produced.astype(jnp.float32), 0.0)
        summed = weighted if summed is None else summed + weighted
    total = lax.psum_scatter(summed, "node", scatter_dimension=0, tiled=True)
    return total.astype(jnp.bfloat16)


def attend(queries, keys, values, incoming_keys, incoming_values, lengths):
    request_rows = queries.shape[0]
    valid_length = keys.shape[1]
    query_groups = QUERY_HEADS // KEY_VALUE_HEADS
    score_scale = 1.0 / math.sqrt(HEAD_WIDTH)
    query_rows = queries.reshape(request_rows, KEY_VALUE_HEADS, query_groups, HEAD_WIDTH)
    stored_keys = keys.reshape(request_rows, valid_length, KEY_VALUE_HEADS, HEAD_WIDTH)
    stored_values = values.reshape(request_rows, valid_length, KEY_VALUE_HEADS, HEAD_WIDTH)
    scores = (
        jnp.einsum("rkgd,rlkd->rkgl", query_rows, stored_keys, preferred_element_type=jnp.float32)
        * score_scale
    )
    new_token_scores = (
        jnp.einsum(
            "behw,bew->beh",
            query_rows,
            incoming_keys.reshape(request_rows, KEY_VALUE_HEADS, HEAD_WIDTH),
            preferred_element_type=jnp.float32,
        )
        * score_scale
    )
    present = (jnp.arange(valid_length, dtype=jnp.int32)[None, :] < lengths[:, None])[
        :, None, None, :
    ]
    masked = jnp.where(present, scores, -1e30)
    highest = jnp.maximum(jnp.max(masked, axis=3), new_token_scores)
    raised = jnp.where(present, jnp.exp(masked - highest[..., None]), 0.0)
    fresh_raised = jnp.exp(new_token_scores - highest)
    denominator = jnp.sum(raised, axis=3) + fresh_raised
    probs = (raised / denominator[..., None]).astype(jnp.bfloat16)
    new_token_probability = (fresh_raised / denominator).astype(jnp.bfloat16)
    blended_output = jnp.einsum(
        "rkgl,rlkd->rkgd", probs, stored_values, preferred_element_type=jnp.float32
    )
    blended_output = blended_output + new_token_probability.astype(jnp.float32)[
        ..., None
    ] * incoming_values.reshape(request_rows, KEY_VALUE_HEADS, 1, HEAD_WIDTH).astype(jnp.float32)
    return blended_output.reshape(request_rows, QUERY_HEADS * HEAD_WIDTH).astype(jnp.bfloat16)


def on_device(
    states,
    norm_gain,
    picks,
    gate_weights,
    w_gate,
    w_up,
    w_down,
    queries,
    keys,
    values,
    incoming_keys,
    incoming_values,
    lengths,
):
    widened = states.astype(jnp.float32)
    meansq = jnp.mean(widened * widened, axis=1, keepdims=True) + 1e-06
    normed = (widened / jnp.sqrt(meansq) * norm_gain[None, :]).astype(jnp.bfloat16)
    experts_all = w_gate.shape[0] * lax.axis_size("node")
    capacity = min(TOK_DEV, max(2, 2 * TOK_DEV * TOPK // experts_all))
    gathered_rows = normed.shape[0] * lax.axis_size("node")
    if gathered_rows <= experts_all * capacity:
        moe_output = dense_block(normed, picks, gate_weights, w_gate, w_up, w_down)
    else:
        moe_output = route_block(normed, picks, gate_weights, w_gate, w_up, w_down, capacity)
    attention_output = attend(queries, keys, values, incoming_keys, incoming_values, lengths)
    return (moe_output, attention_output)


def solution(mesh):
    in_specs = (
        P(("group", "node"), None),
        P(),
        P(("group", "node"), None),
        P(("group", "node"), None),
        P("node", None, None),
        P("node", None, None),
        P("node", None, None),
        P(("group", "node"), None),
        P(("group", "node"), None, None),
        P(("group", "node"), None, None),
        P(("group", "node"), None),
        P(("group", "node"), None),
        P(("group", "node")),
    )
    out_specs = (P(("group", "node"), None), P(("group", "node"), None))
    return jax.shard_map(
        on_device, mesh=mesh, in_specs=in_specs, out_specs=out_specs, check_vma=False
    )
```

profile of v0, /device:TPU:0, one launch (start us, length us, event | category | flops | bytes accessed | tf_op | source)
XLA Modules:
  0.0 130.5 jit_solution(14957401448452033666)
XLA Ops:
  7.2 0.0 copy-start
  7.2 0.0 all-gather.2.cloned.1.call-start
  7.2 1.1 fusion.38
  8.4 1.6 %fusion.40 = bf16[16,2048]{1,0:T(8,128)(2,1)} fusion(bf16[16,2048]{1,0:T(8,128)(2,1)} %param.13, f32[2048]{0:T(1024)} %param.14, f32[16]{0:T(128)S(1)} %add_sqrt_fusion), kind=kLoop, calls=%fused_computation.30 | loop fusion | flops 131072 | bytes 139328 | tf_op jit(solution)/shard_map/convert_element_type | solution.py:147
  9.9 0.0 all-gather.2.cloned.1.call-update
  9.9 0.0 reduce-scatter.2.cloned.1.call-start
  10.0 0.7 reduce_sum.36
  10.7 0.7 broadcast_divide_fusion
  11.4 0.1 copy.28
  11.5 0.8 copy.27
  12.2 0.1 select_reduce_fusion
  12.3 23.5 %all_gather.6 = f32[256,16]{1,0:T(8,128)S(1)} all-gather(f32[16,16]{1,0:T(8,128)S(1)} %select_reduce_fusion), channel_id=1, replica_groups=mesh['group'=2,'node'=16] {'node'}, dimensions={0}, use_global_device_ids=true | all-gather | bytes 17408 | tf_op jit(solution)/shard_map/all_gather | solution.py:71
  35.9 0.2 dynamic-slice_reduce_fusion
  36.0 0.2 compare_reduce_fusion
  36.2 15.2 %all-gather.2.cloned.1.call-done = bf16[256,2048]{1,0:T(8,128)(2,1)} async-done(((bf16[16,2048]{1,0:T(8,128)(2,1)}), bf16[256,2048]{1,0:T(8,128)(2,1)}) %all-gather.2.cloned.1.call-update) | async-done | bytes 1048592 | tf_op jit(solution)/shard_map/all_gather | solution.py:70
  51.5 4.1 %fusion.4 = f32[256,768]{1,0:T(8,128)} fusion(bf16[256,2048]{1,0:T(8,128)(2,1)} %all-gather.2.cloned.1.call-done, bf16[1,2048,768]{2,1,0:T(8,128)(2,1)} %param.17), kind=kOutput, calls=%fused_computation.4 | convolution fusion | flops 805306368 | bytes 4980736 | tf_op jit(solution)/shard_map/dot_general | solution.py:77
  55.5 0.0 copy-done
  55.5 0.0 copy-start.2
  55.5 0.0 copy-start.3
  55.5 0.0 copy-start.4
  55.5 0.0 copy-start.1
  55.6 5.9 %fusion.15 = f32[256,2048]{1,0:T(8,128)} fusion(bf16[1,768,2048]{2,1,0:T(8,128)(2,1)S(1)} %copy-done, f32[256]{0:T(256)S(1)} %dynamic-slice_reduce_fusion, pred[256]{0:T(512)(128)(4,1)S(1)} %compare_reduce_fusion, bf16[256,2048]{1,0:T(8,128)(2,1)} %all-gather.2.cloned.1.call-done, bf16[1,2048,768]{2,1,0:T(8,128)(2,1)} %param.18, f32[256,768]{1,0:T(8,128)} %fusion.4), kind=kOutput, calls=%fused_computation.9 | convolution fusion | flops 1613889536 | bytes 10224896 | tf_op jit(solution)/shard_map/dot_general | solution.py:80
  61.5 0.0 reduce-scatter.2.cloned.1.call-update
  61.5 0.0 copy-done.2
  61.5 0.0 copy-done.3
  61.5 0.0 copy-done.4
  61.5 0.1 iota_compare_fusion.1
  61.6 0.0 copy-done.1
  61.6 0.1 fusion.46
  61.8 1.7 %fusion.55 = (f32[4,4,8]{2,1,0:T(4,128)S(1)}, f32[4,4,8,256]{3,2,1,0:T(8,128)S(1)}) fusion(bf16[1,4,32,128]{3,1,2,0:T(4,128)(2,1)S(1)} %bitcast.60, pred[4,256]{1,0:T(4,128)(4,1)S(1)} %iota_compare_fusion.1, bf16[4,256,512]{2,1,0:T(8,128)(2,1)} %param.21), kind=kOutput, calls=%fused_computation.58 | convolution fusion | flops 8486784 | bytes 1213952 | tf_op jit(solution)/shard_map/rkgd,rlkd->rkgl/dot_general | solution.py:99
  63.5 0.2 fusion.41
  63.7 1.5 %fusion.26 = bf16[1,4,32,128]{3,2,1,0:T(8,128)(2,1)S(1)} fusion(f32[4,4,8,256]{3,2,1,0:T(8,128)S(1)} %get-tuple-element.5, f32[4,4,8]{2,1,0:T(4,128)S(1)} %get-tuple-element.3, f32[4,4,8]{2,1,0:T(4,128)S(1)} %multiply_maximum_fusion, pred[4,256]{1,0:T(4,128)(4,1)S(1)} %iota_compare_fusion.1, f32[4,4,128]{2,1,0:T(4,128)S(1)} %reshape.64, ...), kind=kOutput, calls=%fused_computation.16 | convolution fusion | flops 8568832 | bytes 1223168 | tf_op jit(solution)/shard_map/rkgl,rlkd->rkgd/dot_general | solution.py:121
  65.2 0.6 copy.58
  65.9 56.2 %reduce-scatter.2.cloned.1.call-done = f32[16,2048]{1,0:T(8,128)} async-done(((f32[256,2048]{1,0:T(8,128)}), f32[16,2048]{1,0:T(8,128)}) %reduce-scatter.2.cloned.1.call-update) | async-done | bytes 131088 | tf_op jit(solution)/shard_map/reduce_scatter | solution.py:86
  122.1 1.5 %convert_element_type.49 = bf16[16,2048]{1,0:T(8,128)(2,1)} convert(f32[16,2048]{1,0:T(8,128)} %reduce-scatter.2.cloned.1.call-done) | non-fusion elementwise | flops 32768 | bytes 196608 | tf_op jit(solution)/shard_map/convert_element_type | solution.py:87
  (5 shorter events, 0.1 us)
Async XLA Ops:
  7.2 48.4 %copy-start = (bf16[1,768,2048]{2,1,0:T(8,128)(2,1)S(1)}, bf16[1,768,2048]{2,1,0:T(8,128)(2,1)}, u32[]{:S(2)}) copy-start(bf16[1,768,2048]{2,1,0:T(8,128)(2,1)} %param.19) | copy-start | bytes 9437188
  7.2 44.3 %all-gather.2.cloned.1.call-start = ((), (), s32[]{:S(2)}) async-start(), calls=%async_computation.1 | async-start | bytes 1114112 | tf_op jit(solution)/shard_map/all_gather | solution.py:70
  9.9 112.1 %reduce-scatter.2.cloned.1.call-start = ((), (), s32[]{:S(2)}) async-start(), calls=%async_computation.2 | async-start | bytes 2228224 | tf_op jit(solution)/shard_map/reduce_scatter | solution.py:86
  55.5 6.0 %copy-start.2 = (bf16[4,512]{1,0:T(4,128)(2,1)S(1)}, bf16[4,512]{1,0:T(4,128)(2,1)}, u32[]{:S(2)}) copy-start(bf16[4,512]{1,0:T(4,128)(2,1)} %param.23) | copy-start | bytes 12292
  55.5 6.0 %copy-start.3 = (bf16[4,512]{1,0:T(4,128)(2,1)S(1)}, bf16[4,512]{1,0:T(4,128)(2,1)}, u32[]{:S(2)}) copy-start(bf16[4,512]{1,0:T(4,128)(2,1)} %param.24) | copy-start | bytes 12292
  55.5 6.0 %copy-start.4 = (s32[4]{0:T(128)S(1)}, s32[4]{0:T(128)}, u32[]{:S(2)}) copy-start(s32[4]{0:T(128)} %param.25) | copy-start | bytes 52
  55.5 6.1 %copy-start.1 = (bf16[4,4096]{1,0:T(4,128)(2,1)S(1)}, bf16[4,4096]{1,0:T(4,128)(2,1)}, u32[]{:S(2)}) copy-start(bf16[4,4096]{1,0:T(4,128)(2,1)} %param.20) | copy-start | bytes 98308
Sparse Core Ops, SparseCore 0:
  10.7 40.6 all-gather.1
  61.6 60.4 reduce-scatter.1
where the time goes:
time: 131 us; the launch traced here: 130 us
  waiting for transfers between devices  71.5 us (55%)
  blocking collectives  23.5 us (18%)
  between operations  14.1 us (11%)
  matrix products  13.3 us (10%)
  other arithmetic  6.23 us (5%)
  local copies, waits for them, and re-layouts  1.71 us (1%)
    reduce_scatter x1, waiting for transfers between devices, dense_block(): total = lax.psum_scatter(summed, 'node', scatter_dimension=0, tiled=True)  56.2 us
    all_gather x1, blocking collectives, dense_block(): every_share = lax.all_gather(dense_shares, 'node', axis=0, tiled=True)  23.5 us
    all_gather x1, waiting for transfers between devices, dense_block(): every_row = lax.all_gather(normed, 'node', axis=0, tiled=True)  15.2 us
    dot_general x1, matrix products, dense_block(): jnp.dot(inner, w_down[expert], preferred_element_type=jnp.float32)  5.91 us
    dot_general x1, matrix products, dense_block(): jnp.dot(every_row, w_gate[expert], preferred_element_type=jnp.float32)  4.07 us
  transfers between devices with their start and end apart: 2, of which 2 were waited for; matrix products, arithmetic and copies ran while one was open for 5% of the time, Pallas kernels for 0%

commit v1 on v0

--- a/solution.py
+++ b/solution.py
@@ -9,6 +9,24 @@
 HEAD_WIDTH = 128
 TOPK = 8
 TOK_DEV = 16
+
+
+def gather_around(value, axis, dim):
+    ways, here, step = (lax.axis_size(axis), lax.axis_index(axis), value.shape[dim])
+    shape = [n * ways if d == dim else n for d, n in enumerate(value.shape)]
+    full = lax.dynamic_update_slice_in_dim(
+        jnp.zeros(shape, value.dtype), value, here * step, axis=dim
+    )
+    going_up = going_down = value
+    for far in range(1, ways // 2 + 1):
+        going_up = lax.ppermute(going_up, axis, [(d, (d + 1) % ways) for d in range(ways)])
+        full = lax.dynamic_update_slice_in_dim(full, going_up, (here - far) % ways * step, axis=dim)
+        if 2 * far < ways:
+            going_down = lax.ppermute(going_down, axis, [(d, (d - 1) % ways) for d in range(ways)])
+            full = lax.dynamic_update_slice_in_dim(
+                full, going_down, (here + far) % ways * step, axis=dim
+            )
+    return full
 
 
 def expert_block(received, w_gate, w_up, w_down):
@@ -68,7 +86,7 @@
     chosen = picks[:, :, None] == expert_ids[None, None, :]
     dense_shares = jnp.sum(jnp.where(chosen, shares[:, :, None], 0.0), axis=1)
     every_row = lax.all_gather(normed, "node", axis=0, tiled=True)
-    every_share = lax.all_gather(dense_shares, "node", axis=0, tiled=True)
+    every_share = gather_around(dense_shares, "node", 0)
     own_shares = lax.dynamic_slice_in_dim(
         every_share, node_index * local_experts, local_experts, axis=1
     )

time: 131 us -> 140 us (1.069)
  starting transfers between devices: 0.08 us -> 32.1 us
  blocking collectives: 23.5 us -> 0 us
  local copies, waits for them, and re-layouts: 1.71 us -> 6.56 us
  waiting for transfers between devices: 71.5 us -> 67.1 us
    ppermute x0 -> x15, starting transfers between devices: none -> 32 us  [the longest x7 31.5 us: gather_around(): lax.ppermute(going_down, axis, [(d, (d - 1) % ways) for d in range(ways)])]
    all_gather x1 -> x0, blocking collectives: 23.5 us -> none  [dense_block(): every_share = lax.all_gather(dense_shares, 'node', axis=0, tiled=True)]
    all_gather x1, waiting for transfers between devices: 15.2 us -> 0.02 us  [dense_block(): every_row = lax.all_gather(normed, 'node', axis=0, tiled=True)]
    ppermute x0 -> x15, waiting for transfers between devices: none -> 10.6 us  [the longest x8 10.2 us: gather_around(): lax.ppermute(going_up, axis, [(d, (d + 1) % ways) for d in range(ways)])]
    dynamic_update_slice x0 -> x16, local copies, waits for them, and re-layouts: none -> 3.91 us  [the longest x7 1.9 us: gather_around(): lax.dynamic_update_slice_in_dim(full, going_down, (here + far) % ways * s...]
  transfers between devices with their start and end apart: 2 -> 17, of which waited for: 2 -> 12; matrix products, arithmetic and copies ran while one was open for 5% -> 8% of each run, Pallas kernels for 0% -> 0%
where the time goes in v1:
time: 140 us; the launch traced here: 139 us
  waiting for transfers between devices  67.1 us (48%)
  starting transfers between devices  32.1 us (23%)
  between operations  14.2 us (10%)
  matrix products  13.3 us (10%)
  local copies, waits for them, and re-layouts  6.56 us (5%)
  other arithmetic  6.06 us (4%)
    reduce_scatter x1, waiting for transfers between devices, dense_block(): total = lax.psum_scatter(summed, 'node', scatter_dimension=0, tiled=True)  56.4 us
    ppermute x7, starting transfers between devices, gather_around(): lax.ppermute(going_down, axis, [(d, (d - 1) % ways) for d in range(ways)])  31.5 us
    ppermute x8, waiting for transfers between devices, gather_around(): lax.ppermute(going_up, axis, [(d, (d + 1) % ways) for d in range(ways)])  10.2 us
    dot_general x1, matrix products, dense_block(): jnp.dot(inner, w_down[expert], preferred_element_type=jnp.float32)  5.91 us
    dot_general x1, matrix products, dense_block(): jnp.dot(every_row, w_gate[expert], preferred_element_type=jnp.float32)  4.08 us
  transfers between devices with their start and end apart: 17, of which 12 were waited for; matrix products, arithmetic and copies ran while one was open for 8% of the time, Pallas kernels for 0%

profile of v1, /device:TPU:0, one launch (start us, length us, event | category | flops | bytes accessed | tf_op | source)
XLA Modules:
  0.0 139.4 jit_solution(14283752486971126922)
XLA Ops:
  7.2 1.1 fusion.37
  8.4 1.6 %fusion.39 = bf16[16,2048]{1,0:T(8,128)(2,1)} fusion(bf16[16,2048]{1,0:T(8,128)(2,1)} %param.13, f32[2048]{0:T(1024)} %param.14, f32[16]{0:T(128)S(1)} %add_sqrt_fusion), kind=kLoop, calls=%fused_computation.30 | loop fusion | flops 131072 | bytes 139328 | tf_op jit(solution)/shard_map/convert_element_type | solution.py:165
  10.0 0.7 reduce_sum.36
  10.7 0.7 broadcast_divide_fusion
  11.5 0.8 copy.23
  12.2 0.1 select_reduce_fusion
  12.3 0.5 collective-permute-start
  12.8 5.1 %collective-permute-start.1 = (f32[16,16]{1,0:T(8,128)S(1)}, f32[16,16]{1,0:T(8,128)S(1)}, u32[]{:S(2)}, u32[]{:S(2)}) collective-permute-start(f32[16,16]{1,0:T(8,128)S(1)} %select_reduce_fusion), channel_id=1, source_target_pairs={{0,15},{1,0},{2,1},{3,2},{4,3},{5,4},{6,5},{7,6},{8,7},{9,8},{10,9... | collective-permute-start | bytes 3080 | tf_op jit(solution)/shard_map/ppermute | solution.py:25
  18.0 1.2 collective-permute-done
  19.2 0.1 collective-permute-done.1
  19.3 4.4 %collective-permute-start.3 = (f32[16,16]{1,0:T(8,128)S(1)}, f32[16,16]{1,0:T(8,128)S(1)}, u32[]{:S(2)}, u32[]{:S(2)}) collective-permute-start(f32[16,16]{1,0:T(8,128)S(1)} %collective-permute-done.1), channel_id=1, source_target_pairs={{0,15},{1,0},{2,1},{3,2},{4,3},{5,4},{6,5},{7,6},{8,7},{9,8},{10,9... | collective-permute-start | bytes 3080 | tf_op jit(solution)/shard_map/ppermute | solution.py:25
  23.7 1.3 collective-permute-done.2
  25.0 4.4 %collective-permute-start.5 = (f32[16,16]{1,0:T(8,128)S(1)}, f32[16,16]{1,0:T(8,128)S(1)}, u32[]{:S(2)}, u32[]{:S(2)}) collective-permute-start(f32[16,16]{1,0:T(8,128)S(1)} %collective-permute-done.3), channel_id=1, source_target_pairs={{0,15},{1,0},{2,1},{3,2},{4,3},{5,4},{6,5},{7,6},{8,7},{9,8},{10,9... | collective-permute-start | bytes 3080 | tf_op jit(solution)/shard_map/ppermute | solution.py:25
  29.5 1.3 collective-permute-done.4
  30.8 4.5 %collective-permute-start.7 = (f32[16,16]{1,0:T(8,128)S(1)}, f32[16,16]{1,0:T(8,128)S(1)}, u32[]{:S(2)}, u32[]{:S(2)}) collective-permute-start(f32[16,16]{1,0:T(8,128)S(1)} %collective-permute-done.5), channel_id=1, source_target_pairs={{0,15},{1,0},{2,1},{3,2},{4,3},{5,4},{6,5},{7,6},{8,7},{9,8},{10,9... | collective-permute-start | bytes 3080 | tf_op jit(solution)/shard_map/ppermute | solution.py:25
  35.3 1.2 collective-permute-done.6
  36.5 0.1 collective-permute-done.7
  36.7 4.4 %collective-permute-start.9 = (f32[16,16]{1,0:T(8,128)S(1)}, f32[16,16]{1,0:T(8,128)S(1)}, u32[]{:S(2)}, u32[]{:S(2)}) collective-permute-start(f32[16,16]{1,0:T(8,128)S(1)} %collective-permute-done.7), channel_id=1, source_target_pairs={{0,15},{1,0},{2,1},{3,2},{4,3},{5,4},{6,5},{7,6},{8,7},{9,8},{10,9... | collective-permute-start | bytes 3080 | tf_op jit(solution)/shard_map/ppermute | solution.py:25
  41.1 1.3 collective-permute-done.8
  42.4 4.4 %collective-permute-start.11 = (f32[16,16]{1,0:T(8,128)S(1)}, f32[16,16]{1,0:T(8,128)S(1)}, u32[]{:S(2)}, u32[]{:S(2)}) collective-permute-start(f32[16,16]{1,0:T(8,128)S(1)} %collective-permute-done.9), channel_id=1, source_target_pairs={{0,15},{1,0},{2,1},{3,2},{4,3},{5,4},{6,5},{7,6},{8,7},{9,8},{10,9... | collective-permute-start | bytes 3080 | tf_op jit(solution)/shard_map/ppermute | solution.py:25
  46.8 1.3 collective-permute-done.10
  48.2 0.3 dynamic_update_slice.48
  48.5 0.2 dynamic_update_slice.49
  48.8 0.3 dynamic_update_slice.50
  49.1 0.2 dynamic_update_slice.51
  49.4 0.3 dynamic_update_slice.52
  49.7 4.4 %collective-permute-start.13 = (f32[16,16]{1,0:T(8,128)S(1)}, f32[16,16]{1,0:T(8,128)S(1)}, u32[]{:S(2)}, u32[]{:S(2)}) collective-permute-start(f32[16,16]{1,0:T(8,128)S(1)} %collective-permute-done.11), channel_id=1, source_target_pairs={{0,15},{1,0},{2,1},{3,2},{4,3},{5,4},{6,5},{7,6},{8,7},{9,8},{10,9... | collective-permute-start | bytes 3080 | tf_op jit(solution)/shard_map/ppermute | solution.py:25
  54.2 0.3 dynamic_update_slice.53
  54.5 0.3 dynamic_update_slice.54
  54.9 0.2 dynamic_update_slice.55
  55.2 0.3 dynamic_update_slice.56
  55.5 0.2 dynamic_update_slice.57
  55.8 0.3 dynamic_update_slice.58
  56.1 0.2 dynamic_update_slice.59
  56.4 0.3 dynamic_update_slice.60
  56.8 0.2 dynamic_update_slice.61
  57.1 0.3 dynamic_update_slice.62
  57.4 2.6 %collective-permute-done.14 = f32[16,16]{1,0:T(8,128)S(1)} collective-permute-done((f32[16,16]{1,0:T(8,128)S(1)}, f32[16,16]{1,0:T(8,128)S(1)}, u32[]{:S(2)}, u32[]{:S(2)}) %collective-permute-start.14) | collective-permute-done | bytes 1056 | tf_op jit(solution)/shard_map/ppermute | solution.py:22
  60.0 0.1 dynamic_update_slice.63
  60.2 4.1 %fusion.4 = f32[256,768]{1,0:T(8,128)} fusion(bf16[256,2048]{1,0:T(8,128)(2,1)} %all-gather.2.cloned.1.call-done, bf16[1,2048,768]{2,1,0:T(8,128)(2,1)} %param.17), kind=kOutput, calls=%fused_computation.4 | convolution fusion | flops 805306368 | bytes 4980736 | tf_op jit(solution)/shard_map/dot_general | solution.py:95
  64.3 5.9 %multiply_select_fusion = f32[256,2048]{1,0:T(8,128)} fusion(f32[256]{0:T(256)S(1)} %bitcast.65, pred[256]{0:T(512)(128)(4,1)S(1)} %get-tuple-element.2, bf16[1,768,2048]{2,1,0:T(8,128)(2,1)S(1)} %copy-done, bf16[256,2048]{1,0:T(8,128)(2,1)} %all-gather.2.cloned.1.call-done, bf16[1,2048,768]{2,1,0:T(8,128)(2,1)} %param.18, f32[256,768]{1,0:T(8,128)} %fusion.4), kind=kOutput, calls=%fused_computation.8 | convolution fusion | flops 1613889536 | bytes 10224896 | tf_op jit(solution)/shard_map/dot_general | solution.py:98
  70.3 0.1 fusion.45
  70.5 1.7 %fusion.54 = (f32[4,4,8]{2,1,0:T(4,128)S(1)}, f32[4,4,8,256]{3,2,1,0:T(8,128)S(1)}) fusion(bf16[1,4,32,128]{3,1,2,0:T(4,128)(2,1)S(1)} %bitcast.61, pred[4,256]{1,0:T(4,128)(4,1)S(1)} %iota_compare_fusion.1, bf16[4,256,512]{2,1,0:T(8,128)(2,1)} %param.21), kind=kOutput, calls=%fused_computation.58 | convolution fusion | flops 8486784 | bytes 1213952 | tf_op jit(solution)/shard_map/rkgd,rlkd->rkgl/dot_general | solution.py:117
  72.2 0.2 fusion.40
  72.4 1.5 %fusion.20 = bf16[1,4,32,128]{3,2,1,0:T(8,128)(2,1)S(1)} fusion(f32[4,4,8,256]{3,2,1,0:T(8,128)S(1)} %get-tuple-element.7, f32[4,4,8]{2,1,0:T(4,128)S(1)} %get-tuple-element.5, f32[4,4,8]{2,1,0:T(4,128)S(1)} %multiply_maximum_fusion, pred[4,256]{1,0:T(4,128)(4,1)S(1)} %iota_compare_fusion.1, f32[4,4,128]{2,1,0:T(4,128)S(1)} %reshape.64, ...), kind=kOutput, calls=%fused_computation.15 | convolution fusion | flops 8568832 | bytes 1223168 | tf_op jit(solution)/shard_map/rkgl,rlkd->rkgd/dot_general | solution.py:139
  73.9 0.6 copy.70
  74.6 56.4 %reduce-scatter.2.cloned.1.call-done = f32[16,2048]{1,0:T(8,128)} async-done(((f32[256,2048]{1,0:T(8,128)}), f32[16,2048]{1,0:T(8,128)}) %reduce-scatter.2.cloned.1.call-update) | async-done | bytes 131088 | tf_op jit(solution)/shard_map/reduce_scatter | solution.py:104
  131.0 1.5 %convert_element_type.49 = bf16[16,2048]{1,0:T(8,128)(2,1)} convert(f32[16,2048]{1,0:T(8,128)} %reduce-scatter.2.cloned.1.call-done) | non-fusion elementwise | flops 32768 | bytes 196608 | tf_op jit(solution)/shard_map/convert_element_type | solution.py:105
  (53 shorter events, 1.8 us)
Async XLA Ops:
  7.2 57.1 %copy-start = (bf16[1,768,2048]{2,1,0:T(8,128)(2,1)S(1)}, bf16[1,768,2048]{2,1,0:T(8,128)(2,1)}, u32[]{:S(2)}) copy-start(bf16[1,768,2048]{2,1,0:T(8,128)(2,1)} %param.19) | copy-start | bytes 9437188
  7.2 53.0 %all-gather.2.cloned.1.call-start = ((), (), s32[]{:S(2)}) async-start(), calls=%async_computation.1 | async-start | bytes 1114112 | tf_op jit(solution)/shard_map/all_gather | solution.py:88
  9.9 121.1 %reduce-scatter.2.cloned.1.call-start = ((), (), s32[]{:S(2)}) async-start(), calls=%async_computation.2 | async-start | bytes 2228224 | tf_op jit(solution)/shard_map/reduce_scatter | solution.py:104
  12.3 6.8 %collective-permute-start = (f32[16,16]{1,0:T(8,128)S(1)}, f32[16,16]{1,0:T(8,128)S(1)}, u32[]{:S(2)}, u32[]{:S(2)}) collective-permute-start(f32[16,16]{1,0:T(8,128)S(1)} %select_reduce_fusion), channel_id=1, source_target_pairs={{0,1},{1,2},{2,3},{3,4},{4,5},{5,6},{6,7},{7,8},{8,9},{9,10},{10,1... | collective-permute-start | bytes 3080 | tf_op jit(solution)/shard_map/ppermute | solution.py:22
  12.8 6.4 %collective-permute-start.1 = (f32[16,16]{1,0:T(8,128)S(1)}, f32[16,16]{1,0:T(8,128)S(1)}, u32[]{:S(2)}, u32[]{:S(2)}) collective-permute-start(f32[16,16]{1,0:T(8,128)S(1)} %select_reduce_fusion), channel_id=1, source_target_pairs={{0,15},{1,0},{2,1},{3,2},{4,3},{5,4},{6,5},{7,6},{8,7},{9,8},{10,9... | collective-permute-start | bytes 3080 | tf_op jit(solution)/shard_map/ppermute | solution.py:25
  19.2 5.8 %collective-permute-start.2 = (f32[16,16]{1,0:T(8,128)S(1)}, f32[16,16]{1,0:T(8,128)S(1)}, u32[]{:S(2)}, u32[]{:S(2)}) collective-permute-start(f32[16,16]{1,0:T(8,128)S(1)} %collective-permute-done), channel_id=1, source_target_pairs={{0,1},{1,2},{2,3},{3,4},{4,5},{5,6},{6,7},{7,8},{8,9},{9,10},{10,1... | collective-permute-start | bytes 3080 | tf_op jit(solution)/shard_map/ppermute | solution.py:22
  19.3 5.8 %collective-permute-start.3 = (f32[16,16]{1,0:T(8,128)S(1)}, f32[16,16]{1,0:T(8,128)S(1)}, u32[]{:S(2)}, u32[]{:S(2)}) collective-permute-start(f32[16,16]{1,0:T(8,128)S(1)} %collective-permute-done.1), channel_id=1, source_target_pairs={{0,15},{1,0},{2,1},{3,2},{4,3},{5,4},{6,5},{7,6},{8,7},{9,8},{10,9... | collective-permute-start | bytes 3080 | tf_op jit(solution)/shard_map/ppermute | solution.py:25
  25.0 5.8 %collective-permute-start.4 = (f32[16,16]{1,0:T(8,128)S(1)}, f32[16,16]{1,0:T(8,128)S(1)}, u32[]{:S(2)}, u32[]{:S(2)}) collective-permute-start(f32[16,16]{1,0:T(8,128)S(1)} %collective-permute-done.2), channel_id=1, source_target_pairs={{0,1},{1,2},{2,3},{3,4},{4,5},{5,6},{6,7},{7,8},{8,9},{9,10},{10,1... | collective-permute-start | bytes 3080 | tf_op jit(solution)/shard_map/ppermute | solution.py:22
  25.0 5.8 %collective-permute-start.5 = (f32[16,16]{1,0:T(8,128)S(1)}, f32[16,16]{1,0:T(8,128)S(1)}, u32[]{:S(2)}, u32[]{:S(2)}) collective-permute-start(f32[16,16]{1,0:T(8,128)S(1)} %collective-permute-done.3), channel_id=1, source_target_pairs={{0,15},{1,0},{2,1},{3,2},{4,3},{5,4},{6,5},{7,6},{8,7},{9,8},{10,9... | collective-permute-start | bytes 3080 | tf_op jit(solution)/shard_map/ppermute | solution.py:25
  30.7 5.8 %collective-permute-start.6 = (f32[16,16]{1,0:T(8,128)S(1)}, f32[16,16]{1,0:T(8,128)S(1)}, u32[]{:S(2)}, u32[]{:S(2)}) collective-permute-start(f32[16,16]{1,0:T(8,128)S(1)} %collective-permute-done.4), channel_id=1, source_target_pairs={{0,1},{1,2},{2,3},{3,4},{4,5},{5,6},{6,7},{7,8},{8,9},{9,10},{10,1... | collective-permute-start | bytes 3080 | tf_op jit(solution)/shard_map/ppermute | solution.py:22
  30.8 5.8 %collective-permute-start.7 = (f32[16,16]{1,0:T(8,128)S(1)}, f32[16,16]{1,0:T(8,128)S(1)}, u32[]{:S(2)}, u32[]{:S(2)}) collective-permute-start(f32[16,16]{1,0:T(8,128)S(1)} %collective-permute-done.5), channel_id=1, source_target_pairs={{0,15},{1,0},{2,1},{3,2},{4,3},{5,4},{6,5},{7,6},{8,7},{9,8},{10,9... | collective-permute-start | bytes 3080 | tf_op jit(solution)/shard_map/ppermute | solution.py:25
  36.5 5.9 %collective-permute-start.8 = (f32[16,16]{1,0:T(8,128)S(1)}, f32[16,16]{1,0:T(8,128)S(1)}, u32[]{:S(2)}, u32[]{:S(2)}) collective-permute-start(f32[16,16]{1,0:T(8,128)S(1)} %collective-permute-done.6), channel_id=1, source_target_pairs={{0,1},{1,2},{2,3},{3,4},{4,5},{5,6},{6,7},{7,8},{8,9},{9,10},{10,1... | collective-permute-start | bytes 3080 | tf_op jit(solution)/shard_map/ppermute | solution.py:22
  36.7 5.8 %collective-permute-start.9 = (f32[16,16]{1,0:T(8,128)S(1)}, f32[16,16]{1,0:T(8,128)S(1)}, u32[]{:S(2)}, u32[]{:S(2)}) collective-permute-start(f32[16,16]{1,0:T(8,128)S(1)} %collective-permute-done.7), channel_id=1, source_target_pairs={{0,15},{1,0},{2,1},{3,2},{4,3},{5,4},{6,5},{7,6},{8,7},{9,8},{10,9... | collective-permute-start | bytes 3080 | tf_op jit(solution)/shard_map/ppermute | solution.py:25
  42.4 5.8 %collective-permute-start.10 = (f32[16,16]{1,0:T(8,128)S(1)}, f32[16,16]{1,0:T(8,128)S(1)}, u32[]{:S(2)}, u32[]{:S(2)}) collective-permute-start(f32[16,16]{1,0:T(8,128)S(1)} %collective-permute-done.8), channel_id=1, source_target_pairs={{0,1},{1,2},{2,3},{3,4},{4,5},{5,6},{6,7},{7,8},{8,9},{9,10},{10,1... | collective-permute-start | bytes 3080 | tf_op jit(solution)/shard_map/ppermute | solution.py:22
  42.4 7.3 %collective-permute-start.11 = (f32[16,16]{1,0:T(8,128)S(1)}, f32[16,16]{1,0:T(8,128)S(1)}, u32[]{:S(2)}, u32[]{:S(2)}) collective-permute-start(f32[16,16]{1,0:T(8,128)S(1)} %collective-permute-done.9), channel_id=1, source_target_pairs={{0,15},{1,0},{2,1},{3,2},{4,3},{5,4},{6,5},{7,6},{8,7},{9,8},{10,9... | collective-permute-start | bytes 3080 | tf_op jit(solution)/shard_map/ppermute | solution.py:25
  48.2 6.0 %collective-permute-start.12 = (f32[16,16]{1,0:T(8,128)S(1)}, f32[16,16]{1,0:T(8,128)S(1)}, u32[]{:S(2)}, u32[]{:S(2)}) collective-permute-start(f32[16,16]{1,0:T(8,128)S(1)} %collective-permute-done.10), channel_id=1, source_target_pairs={{0,1},{1,2},{2,3},{3,4},{4,5},{5,6},{6,7},{7,8},{8,9},{9,10},{10,1... | collective-permute-start | bytes 3080 | tf_op jit(solution)/shard_map/ppermute | solution.py:22
  49.7 7.3 %collective-permute-start.13 = (f32[16,16]{1,0:T(8,128)S(1)}, f32[16,16]{1,0:T(8,128)S(1)}, u32[]{:S(2)}, u32[]{:S(2)}) collective-permute-start(f32[16,16]{1,0:T(8,128)S(1)} %collective-permute-done.11), channel_id=1, source_target_pairs={{0,15},{1,0},{2,1},{3,2},{4,3},{5,4},{6,5},{7,6},{8,7},{9,8},{10,9... | collective-permute-start | bytes 3080 | tf_op jit(solution)/shard_map/ppermute | solution.py:25
  54.2 5.8 %collective-permute-start.14 = (f32[16,16]{1,0:T(8,128)S(1)}, f32[16,16]{1,0:T(8,128)S(1)}, u32[]{:S(2)}, u32[]{:S(2)}) collective-permute-start(f32[16,16]{1,0:T(8,128)S(1)} %collective-permute-done.12), channel_id=1, source_target_pairs={{0,1},{1,2},{2,3},{3,4},{4,5},{5,6},{6,7},{7,8},{8,9},{9,10},{10,1... | collective-permute-start | bytes 3080 | tf_op jit(solution)/shard_map/ppermute | solution.py:22
  64.2 6.0 %copy-start.2 = (bf16[4,512]{1,0:T(4,128)(2,1)S(1)}, bf16[4,512]{1,0:T(4,128)(2,1)}, u32[]{:S(2)}) copy-start(bf16[4,512]{1,0:T(4,128)(2,1)} %param.23) | copy-start | bytes 12292
  64.3 6.0 %copy-start.3 = (bf16[4,512]{1,0:T(4,128)(2,1)S(1)}, bf16[4,512]{1,0:T(4,128)(2,1)}, u32[]{:S(2)}) copy-start(bf16[4,512]{1,0:T(4,128)(2,1)} %param.24) | copy-start | bytes 12292
  64.3 6.0 %copy-start.4 = (s32[4]{0:T(128)S(1)}, s32[4]{0:T(128)}, u32[]{:S(2)}) copy-start(s32[4]{0:T(128)} %param.25) | copy-start | bytes 52
  64.3 6.1 %copy-start.1 = (bf16[4,4096]{1,0:T(4,128)(2,1)S(1)}, bf16[4,4096]{1,0:T(4,128)(2,1)}, u32[]{:S(2)}) copy-start(bf16[4,4096]{1,0:T(4,128)(2,1)} %param.20) | copy-start | bytes 98308
Sparse Core Ops, SparseCore 0:
  10.7 40.7 all-gather.1
  70.3 60.6 reduce-scatter.1
